TPU v7x, 256 devices: a whole 4x4x8 slice. The times are simulated.
256 devices in a mesh: ctx: 64 (over y_lo, z, x), fsdp: 4 (over y_hi, core).
Axes of the slice: x: 4, y: 4 (y_hi: 2, y_lo: 2; y = y_hi * 2 + y_lo), z: 8, core: 2. Of those that a mesh axis runs over, the one named last changes fastest.
Arguments:
- query: bfloat16 [16384, 2048], P('ctx', 'fsdp'), may hold values from -11 to 11
- key: bfloat16 [16384, 2048], P('ctx', 'fsdp'), may hold values from -11 to 11
- value: bfloat16 [16384, 2048], P('ctx', 'fsdp'), may hold values from -6 to 6
- doc_ids: int32 [16384], P('ctx'), may hold values from 0 to 19, never falling along the last dimension, each value on 1 to 2048 neighbouring positions
- out_weight: bfloat16 [2048, 4096], P(('fsdp', 'ctx')), may hold values from -0.125 to 0.125
- grad_out: bfloat16 [16384, 4096], P('ctx', 'fsdp'), may hold values from -6 to 6
Outputs:
- grad_query: bfloat16 [16384, 2048], P('ctx', 'fsdp')
- grad_key: bfloat16 [16384, 2048], P('ctx', 'fsdp')
- grad_value: bfloat16 [16384, 2048], P('ctx', 'fsdp')
- grad_out_weight: float32 [2048, 4096], P(('fsdp', 'ctx'))
Inputs may be any that keep to these rules, and one draw needn't show every extreme that they name: `doc_ids`: document ids never fall along the sequence; every document has 1 to 2048 tokens and one has exactly 2048.
All inputs are finite; a program needn't handle non-finite values.
Results may differ from a plain program's by a relative error of at most 0.034.
Values may be sent and summed in bfloat16 or wider, within the bound.
No kernel may reach another device: no remote copies, remote signals or barrier semaphores. Data moves between devices by JAX's collectives and lax.ppermute only.
A program may use at most 128 MiB of HBM per device.

v0:
```python
import math
import jax
import jax.numpy as jnp
from jax import lax
from jax.sharding import PartitionSpec as P

DH = 128
NEGATIVE = -1e30


def shifted(array, axis, by):
    devices = lax.axis_size(axis)
    pairs = [(i, i + by) for i in range(devices) if 0 <= i + by < devices]
    return lax.ppermute(array, axis, pairs)


def as_sent(array):

    def short(part):
        return part.astype(jnp.bfloat16) if part.dtype == jnp.float32 else part

    return jax.tree.map(short, array)


def passed_along(block, axis, distance):
    devices = range(lax.axis_size(axis))
    route = [((i - distance) % len(devices), i) for i in devices]
    return lax.ppermute(block, axis, route)


def shards(query, key, value, doc_ids, out_weight, grad_out):
    tok_rows = query.shape[0]
    feature_width = query.shape[1]
    head_count = feature_width // DH
    cycle_size = lax.axis_size("ctx")
    cycle_reach = max(cycle_size // 8, 2)
    cycle_index = lax.axis_index("ctx")
    score_scale = 1.0 / math.sqrt(DH)
    local_pos = jnp.arange(tok_rows, dtype=jnp.int32)
    own_pos = cycle_index * tok_rows + local_pos
    own_docs = doc_ids + 1
    query_heads = query.reshape(tok_rows, head_count, DH)
    key_heads = key.reshape(tok_rows, head_count, DH)
    value_heads = value.reshape(tok_rows, head_count, DH)

    def scores_of(query_block, key_block):
        return (
            jnp.einsum("tnd,snd->nts", query_block, key_block, preferred_element_type=jnp.float32)
            * score_scale
        )

    state = (
        jnp.full((head_count, tok_rows), NEGATIVE, jnp.float32),
        jnp.zeros((head_count, tok_rows), jnp.float32),
        jnp.zeros((head_count, tok_rows, DH), jnp.float32),
    )
    key_block, value_block = (key_heads, value_heads)
    key_docs = own_docs
    stored_blocks = []
    for cycle_step in range(cycle_reach + 1):
        if cycle_step > 0:
            key_block, value_block = shifted((key_block, value_block), "ctx", 1)
            key_docs = shifted(key_docs, "ctx", 1)
        key_pos = own_pos - cycle_step * tok_rows
        pair_mask = (own_docs[:, None] == key_docs[None, :]) & (
            key_pos[None, :] <= own_pos[:, None]
        )
        forward_row_max, forward_row_sum, forward_output_sum = state
        forward_scores = jnp.where(pair_mask[None], scores_of(query_heads, key_block), NEGATIVE)
        new_max = jnp.maximum(forward_row_max, jnp.max(forward_scores, axis=-1))
        decay_factor = jnp.exp(forward_row_max - new_max)
        forward_weights = jnp.where(
            pair_mask[None], jnp.exp(forward_scores - new_max[..., None]), 0.0
        )
        new_sum = forward_row_sum * decay_factor + jnp.sum(forward_weights, axis=-1)
        weights_low = forward_weights.astype(jnp.bfloat16)
        new_output = forward_output_sum * decay_factor[..., None] + jnp.einsum(
            "nts,snd->ntd", weights_low, value_block, preferred_element_type=jnp.float32
        )
        state = (new_max, new_sum, new_output)
        stored_blocks.append((key_block, value_block, pair_mask))
    row_max, row_sum, output_sum = state
    log_total = row_max + jnp.log(row_sum)
    attn_heads = (output_sum / row_sum[..., None]).astype(jnp.bfloat16).transpose(1, 0, 2)
    attention = attn_heads.reshape(tok_rows, feature_width)
    grad_full = lax.all_gather(grad_out, "fsdp", axis=1, tiled=True)
    grad_attn = lax.dot_general(
        grad_full,
        lax.all_gather(out_weight, "ctx", axis=0, tiled=True),
        (((1,), (1,)), ((), ())),
        preferred_element_type=jnp.float32,
    ).astype(jnp.bfloat16)
    grad_weight = lax.psum_scatter(
        lax.dot_general(
            attention, grad_full, (((0,), (0,)), ((), ())), preferred_element_type=jnp.float32
        ),
        "ctx",
        scatter_dimension=0,
        tiled=True,
    )
    grad_heads = grad_attn.reshape(tok_rows, head_count, DH)
    delta_sum = jnp.einsum(
        "tnd,tnd->nt", grad_heads, attn_heads, preferred_element_type=jnp.float32
    )
    grad_query = jnp.zeros((tok_rows, head_count, DH), jnp.float32)
    carried = None
    for cycle_step in range(cycle_reach + 1):
        key_block, value_block, pair_mask = stored_blocks[cycle_step]
        if cycle_step > 0:
            carried = jax.tree.map(
                lambda part, own: part.astype(own.dtype),
                passed_along(as_sent(carried), "ctx", 1),
                carried,
            )
        scores = scores_of(query_heads, key_block)
        weights = jnp.where(pair_mask[None], jnp.exp(scores - log_total[..., None]), 0.0)
        rounded = weights.astype(jnp.bfloat16)
        value_part = jnp.einsum(
            "nts,tnd->snd", rounded, grad_heads, preferred_element_type=jnp.float32
        )
        grad_weights = jnp.einsum(
            "tnd,snd->nts", grad_heads, value_block, preferred_element_type=jnp.float32
        )
        grad_scores = (weights * (grad_weights - delta_sum[..., None])).astype(jnp.bfloat16)
        query_part = (
            jnp.einsum("nts,snd->tnd", grad_scores, key_block, preferred_element_type=jnp.float32)
            * score_scale
        )
        key_part = (
            jnp.einsum("nts,tnd->snd", grad_scores, query_heads, preferred_element_type=jnp.float32)
            * score_scale
        )
        query_part, key_part, value_part = (query_part, key_part, value_part)
        grad_query = grad_query + query_part
        if cycle_step == 0:
            carried = (key_part, value_part)
        else:
            carried = (carried[0] + key_part, carried[1] + value_part)
    grad_key, grad_value = jax.tree.map(
        lambda part, own: part.astype(own.dtype),
        passed_along(as_sent(carried), "ctx", -cycle_reach),
        carried,
    )
    return (
        grad_query.reshape(tok_rows, feature_width).astype(jnp.bfloat16),
        grad_key.reshape(tok_rows, feature_width).astype(jnp.bfloat16),
        grad_value.reshape(tok_rows, feature_width).astype(jnp.bfloat16),
        grad_weight,
    )


def solution(mesh):
    return jax.shard_map(
        shards,
        mesh=mesh,
        in_specs=(
            P("ctx", "fsdp"),
            P("ctx", "fsdp"),
            P("ctx", "fsdp"),
            P("ctx"),
            P(("fsdp", "ctx"), None),
            P("ctx", "fsdp"),
        ),
        out_specs=(P("ctx", "fsdp"), P("ctx", "fsdp"), P("ctx", "fsdp"), P(("fsdp", "ctx"), None)),
        check_vma=False,
    )
```

profile of v0, /device:TPU:8, one launch (start us, length us, event | category | flops | bytes accessed | tf_op | source)
XLA Modules:
  0.0 712.0 jit_solution(2859584681869793939)
XLA Ops:
  12.8 8.0 %collective-permute-done = s32[256]{0:T(256)S(1)} collective-permute-done((s32[256]{0:T(256)S(1)}, s32[256]{0:T(256)S(1)}, u32[]{:S(2)}, u32[]{:S(2)}) %collective-permute-start) | collective-permute-done | bytes 1056 | tf_op jit(solution)/shard_map/ppermute | solution.py:14
  22.7 7.8 %collective-permute-done.2 = s32[256]{0:T(256)S(1)} collective-permute-done((s32[256]{0:T(256)S(1)}, s32[256]{0:T(256)S(1)}, u32[]{:S(2)}, u32[]{:S(2)}) %collective-permute-start.2) | collective-permute-done | bytes 1056 | tf_op jit(solution)/shard_map/ppermute | solution.py:14
  42.1 9.6 %collective-permute-done.6 = s32[256]{0:T(256)S(1)} collective-permute-done((s32[256]{0:T(256)S(1)}, s32[256]{0:T(256)S(1)}, u32[]{:S(2)}, u32[]{:S(2)}) %collective-permute-start.6) | collective-permute-done | bytes 1056 | tf_op jit(solution)/shard_map/ppermute | solution.py:14
  53.6 7.7 %collective-permute-done.8 = s32[256]{0:T(256)S(1)} collective-permute-done((s32[256]{0:T(256)S(1)}, s32[256]{0:T(256)S(1)}, u32[]{:S(2)}, u32[]{:S(2)}) %collective-permute-start.8) | collective-permute-done | bytes 1056 | tf_op jit(solution)/shard_map/ppermute | solution.py:14
  63.3 7.8 %collective-permute-done.10 = s32[256]{0:T(256)S(1)} collective-permute-done((s32[256]{0:T(256)S(1)}, s32[256]{0:T(256)S(1)}, u32[]{:S(2)}, u32[]{:S(2)}) %collective-permute-start.10) | collective-permute-done | bytes 1056 | tf_op jit(solution)/shard_map/ppermute | solution.py:14
  73.0 7.7 %collective-permute-done.12 = s32[256]{0:T(256)S(1)} collective-permute-done((s32[256]{0:T(256)S(1)}, s32[256]{0:T(256)S(1)}, u32[]{:S(2)}, u32[]{:S(2)}) %collective-permute-start.12) | collective-permute-done | bytes 1056 | tf_op jit(solution)/shard_map/ppermute | solution.py:14
  82.6 7.7 %collective-permute-done.14 = s32[256]{0:T(256)S(1)} collective-permute-done((s32[256]{0:T(256)S(1)}, s32[256]{0:T(256)S(1)}, u32[]{:S(2)}, u32[]{:S(2)}) %collective-permute-start.14) | collective-permute-done | bytes 1056 | tf_op jit(solution)/shard_map/ppermute | solution.py:14
  95.9 9.4 %collective-permute-done.3 = bf16[256,4,128]{2,0,1:T(8,128)(2,1)S(1)} collective-permute-done((bf16[256,4,128]{2,0,1:T(8,128)(2,1)S(1)}, bf16[256,4,128]{2,0,1:T(8,128)(2,1)S(1)}, u32[]{:S(2)}, u32[]{:S(2)}) %collective-permute-start.3) | collective-permute-done | bytes 262176 | tf_op jit(solution)/shard_map/ppermute | solution.py:14
  120.5 7.6 %collective-permute-done.18 = bf16[256,4,128]{0,2,1:T(8,128)(2,1)S(1)} collective-permute-done((bf16[256,4,128]{0,2,1:T(8,128)(2,1)S(1)}, bf16[256,4,128]{0,2,1:T(8,128)(2,1)S(1)}, u32[]{:S(2)}, u32[]{:S(2)}) %collective-permute-start.18) | collective-permute-done | bytes 262176 | tf_op jit(solution)/shard_map/ppermute | solution.py:14
  135.9 6.3 collective-permute-done.19
  157.4 7.1 %collective-permute-done.11 = bf16[256,4,128]{2,0,1:T(8,128)(2,1)S(1)} collective-permute-done((bf16[256,4,128]{2,0,1:T(8,128)(2,1)S(1)}, bf16[256,4,128]{2,0,1:T(8,128)(2,1)S(1)}, u32[]{:S(2)}, u32[]{:S(2)}) %collective-permute-start.11) | collective-permute-done | bytes 262176 | tf_op jit(solution)/shard_map/ppermute | solution.py:14
  172.7 6.6 collective-permute-done.13
  201.0 145.4 %all-gather.5.cloned.1.call-done = bf16[512,4096]{1,0:T(8,128)(2,1)} async-done(((bf16[8,4096]{1,0:T(8,128)(2,1)}), bf16[512,4096]{1,0:T(8,128)(2,1)}) %all-gather.5.cloned.1.call-update) | async-done | bytes 4194320 | tf_op jit(solution)/shard_map/all_gather | solution.py:89
  382.2 6.9 collective-permute-done.33
  389.9 8.2 %collective-permute-done.25 = bf16[256,4,128]{0,2,1:T(8,128)(2,1)S(1)} collective-permute-done((bf16[256,4,128]{0,2,1:T(8,128)(2,1)S(1)}, bf16[256,4,128]{0,2,1:T(8,128)(2,1)S(1)}, u32[]{:S(2)}, u32[]{:S(2)}) %collective-permute-start.25) | collective-permute-done | bytes 262176 | tf_op jit(solution)/shard_map/ppermute | solution.py:28
  398.2 8.1 %collective-permute-done.34 = bf16[256,4,128]{0,2,1:T(8,128)(2,1)S(1)} collective-permute-done((bf16[256,4,128]{0,2,1:T(8,128)(2,1)S(1)}, bf16[256,4,128]{0,2,1:T(8,128)(2,1)S(1)}, u32[]{:S(2)}, u32[]{:S(2)}) %collective-permute-start.34) | collective-permute-done | bytes 262176 | tf_op jit(solution)/shard_map/ppermute | solution.py:28
  407.1 6.8 collective-permute-done.26
  414.0 7.5 %collective-permute-done.35 = bf16[256,4,128]{0,2,1:T(8,128)(2,1)S(1)} collective-permute-done((bf16[256,4,128]{0,2,1:T(8,128)(2,1)S(1)}, bf16[256,4,128]{0,2,1:T(8,128)(2,1)S(1)}, u32[]{:S(2)}, u32[]{:S(2)}) %collective-permute-start.35) | collective-permute-done | bytes 262176 | tf_op jit(solution)/shard_map/ppermute | solution.py:28
  422.3 6.5 collective-permute-done.27
  433.8 7.6 %collective-permute-done.28 = bf16[256,4,128]{0,2,1:T(8,128)(2,1)S(1)} collective-permute-done((bf16[256,4,128]{0,2,1:T(8,128)(2,1)S(1)}, bf16[256,4,128]{0,2,1:T(8,128)(2,1)S(1)}, u32[]{:S(2)}, u32[]{:S(2)}) %collective-permute-start.28) | collective-permute-done | bytes 262176 | tf_op jit(solution)/shard_map/ppermute | solution.py:28
  445.7 7.2 %collective-permute-done.29 = bf16[256,4,128]{0,2,1:T(8,128)(2,1)S(1)} collective-permute-done((bf16[256,4,128]{0,2,1:T(8,128)(2,1)S(1)}, bf16[256,4,128]{0,2,1:T(8,128)(2,1)S(1)}, u32[]{:S(2)}, u32[]{:S(2)}) %collective-permute-start.29) | collective-permute-done | bytes 262176 | tf_op jit(solution)/shard_map/ppermute | solution.py:28
  457.8 6.4 collective-permute-done.30
  484.6 6.3 collective-permute-done.41
  491.8 213.5 %reduce-scatter.2.cloned.1.call-done = f32[8,4096]{1,0:T(8,128)} async-done(((f32[512,4096]{1,0:T(8,128)}), f32[8,4096]{1,0:T(8,128)}) %reduce-scatter.2.cloned.1.call-update) | async-done | bytes 131088 | tf_op jit(solution)/shard_map/reduce_scatter | solution.py:93
  (352 shorter events, 172.4 us)
Async XLA Ops:
  7.2 193.8 %all-gather.3.cloned.1.call-start = ((), (), s32[]{:S(2)}) async-start(), calls=%async_computation.1 | async-start | bytes 2621440 | tf_op jit(solution)/shard_map/all_gather | solution.py:86
  7.9 338.5 %all-gather.5.cloned.1.call-start = ((), (), s32[]{:S(2)}) async-start(), calls=%async_computation.2 | async-start | bytes 4259840 | tf_op jit(solution)/shard_map/all_gather | solution.py:89
  8.7 696.6 %reduce-scatter.2.cloned.1.call-start = ((), (), s32[]{:S(2)}) async-start(), calls=%async_computation.3 | async-start | bytes 8519680 | tf_op jit(solution)/shard_map/reduce_scatter | solution.py:93
  33.6 58.0 %collective-permute-start.1 = (bf16[256,4,128]{2,0,1:T(8,128)(2,1)S(1)}, bf16[256,4,128]{2,0,1:T(8,128)(2,1)S(1)}, u32[]{:S(2)}, u32[]{:S(2)}) collective-permute-start(bf16[256,4,128]{2,0,1:T(8,128)(2,1)S(1)} %copy.116), channel_id=1, source_target_pairs={{0,4},{4,8},{8,12},{12,16},{16,20},{20,24},{24,28},{28,32},{32,36}... | collective-permute-start | bytes 786440 | tf_op jit(solution)/shard_map/ppermute | solution.py:14
  36.7 56.9 %collective-permute-start.16 = (bf16[256,4,128]{0,2,1:T(8,128)(2,1)S(1)}, bf16[256,4,128]{0,2,1:T(8,128)(2,1)S(1)}, u32[]{:S(2)}, u32[]{:S(2)}) collective-permute-start(bf16[256,4,128]{0,2,1:T(8,128)(2,1)S(1)} %bitcast.466), channel_id=1, source_target_pairs={{0,4},{4,8},{8,12},{12,16},{16,20},{20,24},{24,28},{28,32},{32,36}... | collective-permute-start | bytes 786440 | tf_op jit(solution)/shard_map/ppermute | solution.py:14
  91.7 13.6 %collective-permute-start.3 = (bf16[256,4,128]{2,0,1:T(8,128)(2,1)S(1)}, bf16[256,4,128]{2,0,1:T(8,128)(2,1)S(1)}, u32[]{:S(2)}, u32[]{:S(2)}) collective-permute-start(bf16[256,4,128]{2,0,1:T(8,128)(2,1)S(1)} %collective-permute-done.1), channel_id=1, source_target_pairs={{0,4},{4,8},{8,12},{12,16},{16,20},{20,24},{24,28},{28,32},{32,36}... | collective-permute-start | bytes 786440 | tf_op jit(solution)/shard_map/ppermute | solution.py:14
  93.6 17.8 %collective-permute-start.17 = (bf16[256,4,128]{0,2,1:T(8,128)(2,1)S(1)}, bf16[256,4,128]{0,2,1:T(8,128)(2,1)S(1)}, u32[]{:S(2)}, u32[]{:S(2)}) collective-permute-start(bf16[256,4,128]{0,2,1:T(8,128)(2,1)S(1)} %collective-permute-done.16), channel_id=1, source_target_pairs={{0,4},{4,8},{8,12},{12,16},{16,20},{20,24},{24,28},{28,32},{32,36}... | collective-permute-start | bytes 786440 | tf_op jit(solution)/shard_map/ppermute | solution.py:14
  105.3 13.3 %collective-permute-start.5 = (bf16[256,4,128]{2,0,1:T(8,128)(2,1)S(1)}, bf16[256,4,128]{2,0,1:T(8,128)(2,1)S(1)}, u32[]{:S(2)}, u32[]{:S(2)}) collective-permute-start(bf16[256,4,128]{2,0,1:T(8,128)(2,1)S(1)} %collective-permute-done.3), channel_id=1, source_target_pairs={{0,4},{4,8},{8,12},{12,16},{16,20},{20,24},{24,28},{28,32},{32,36}... | collective-permute-start | bytes 786440 | tf_op jit(solution)/shard_map/ppermute | solution.py:14
  111.4 16.6 %collective-permute-start.18 = (bf16[256,4,128]{0,2,1:T(8,128)(2,1)S(1)}, bf16[256,4,128]{0,2,1:T(8,128)(2,1)S(1)}, u32[]{:S(2)}, u32[]{:S(2)}) collective-permute-start(bf16[256,4,128]{0,2,1:T(8,128)(2,1)S(1)} %collective-permute-done.17), channel_id=1, source_target_pairs={{0,4},{4,8},{8,12},{12,16},{16,20},{20,24},{24,28},{28,32},{32,36}... | collective-permute-start | bytes 786440 | tf_op jit(solution)/shard_map/ppermute | solution.py:14
  118.6 15.4 %collective-permute-start.7 = (bf16[256,4,128]{2,0,1:T(8,128)(2,1)S(1)}, bf16[256,4,128]{2,0,1:T(8,128)(2,1)S(1)}, u32[]{:S(2)}, u32[]{:S(2)}) collective-permute-start(bf16[256,4,128]{2,0,1:T(8,128)(2,1)S(1)} %collective-permute-done.5), channel_id=1, source_target_pairs={{0,4},{4,8},{8,12},{12,16},{16,20},{20,24},{24,28},{28,32},{32,36}... | collective-permute-start | bytes 786440 | tf_op jit(solution)/shard_map/ppermute | solution.py:14
  128.0 14.1 %collective-permute-start.19 = (bf16[256,4,128]{0,2,1:T(8,128)(2,1)S(1)}, bf16[256,4,128]{0,2,1:T(8,128)(2,1)S(1)}, u32[]{:S(2)}, u32[]{:S(2)}) collective-permute-start(bf16[256,4,128]{0,2,1:T(8,128)(2,1)S(1)} %collective-permute-done.18), channel_id=1, source_target_pairs={{0,4},{4,8},{8,12},{12,16},{16,20},{20,24},{24,28},{28,32},{32,36}... | collective-permute-start | bytes 786440 | tf_op jit(solution)/shard_map/ppermute | solution.py:14
  134.0 15.4 %collective-permute-start.9 = (bf16[256,4,128]{2,0,1:T(8,128)(2,1)S(1)}, bf16[256,4,128]{2,0,1:T(8,128)(2,1)S(1)}, u32[]{:S(2)}, u32[]{:S(2)}) collective-permute-start(bf16[256,4,128]{2,0,1:T(8,128)(2,1)S(1)} %collective-permute-done.7), channel_id=1, source_target_pairs={{0,4},{4,8},{8,12},{12,16},{16,20},{20,24},{24,28},{28,32},{32,36}... | collective-permute-start | bytes 786440 | tf_op jit(solution)/shard_map/ppermute | solution.py:14
  149.3 15.2 %collective-permute-start.11 = (bf16[256,4,128]{2,0,1:T(8,128)(2,1)S(1)}, bf16[256,4,128]{2,0,1:T(8,128)(2,1)S(1)}, u32[]{:S(2)}, u32[]{:S(2)}) collective-permute-start(bf16[256,4,128]{2,0,1:T(8,128)(2,1)S(1)} %collective-permute-done.9), channel_id=1, source_target_pairs={{0,4},{4,8},{8,12},{12,16},{16,20},{20,24},{24,28},{28,32},{32,36}... | collective-permute-start | bytes 786440 | tf_op jit(solution)/shard_map/ppermute | solution.py:14
  155.2 15.3 %collective-permute-start.21 = (bf16[256,4,128]{0,2,1:T(8,128)(2,1)S(1)}, bf16[256,4,128]{0,2,1:T(8,128)(2,1)S(1)}, u32[]{:S(2)}, u32[]{:S(2)}) collective-permute-start(bf16[256,4,128]{0,2,1:T(8,128)(2,1)S(1)} %collective-permute-done.20), channel_id=1, source_target_pairs={{0,4},{4,8},{8,12},{12,16},{16,20},{20,24},{24,28},{28,32},{32,36}... | collective-permute-start | bytes 786440 | tf_op jit(solution)/shard_map/ppermute | solution.py:14
  164.6 14.8 %collective-permute-start.13 = (bf16[256,4,128]{2,0,1:T(8,128)(2,1)S(1)}, bf16[256,4,128]{2,0,1:T(8,128)(2,1)S(1)}, u32[]{:S(2)}, u32[]{:S(2)}) collective-permute-start(bf16[256,4,128]{2,0,1:T(8,128)(2,1)S(1)} %collective-permute-done.11), channel_id=1, source_target_pairs={{0,4},{4,8},{8,12},{12,16},{16,20},{20,24},{24,28},{28,32},{32,36}... | collective-permute-start | bytes 786440 | tf_op jit(solution)/shard_map/ppermute | solution.py:14
  170.5 16.4 %collective-permute-start.22 = (bf16[256,4,128]{0,2,1:T(8,128)(2,1)S(1)}, bf16[256,4,128]{0,2,1:T(8,128)(2,1)}, u32[]{:S(2)}, u32[]{:S(2)}) collective-permute-start(bf16[256,4,128]{0,2,1:T(8,128)(2,1)S(1)} %collective-permute-done.21), channel_id=1, source_target_pairs={{0,4},{4,8},{8,12},{12,16},{16,20},{20,24},{24,28},{28,32},{32,36}... | collective-permute-start | bytes 786440 | tf_op jit(solution)/shard_map/ppermute | solution.py:14
  186.9 169.9 %collective-permute-start.23 = (bf16[256,4,128]{0,2,1:T(8,128)(2,1)}, bf16[256,4,128]{0,2,1:T(8,128)(2,1)}, u32[]{:S(2)}, u32[]{:S(2)}) collective-permute-start(bf16[256,4,128]{0,2,1:T(8,128)(2,1)} %collective-permute-done.22), channel_id=1, source_target_pairs={{0,4},{4,8},{8,12},{12,16},{16,20},{20,24},{24,28},{28,32},{32,36}... | collective-permute-start | bytes 786440 | tf_op jit(solution)/shard_map/ppermute | solution.py:14
  366.9 14.9 %collective-permute-start.24 = (bf16[256,4,128]{0,2,1:T(8,128)(2,1)S(1)}, bf16[256,4,128]{0,2,1:T(8,128)(2,1)S(1)}, u32[]{:S(2)}, u32[]{:S(2)}) collective-permute-start(bf16[256,4,128]{0,2,1:T(8,128)(2,1)S(1)} %fusion.49), channel_id=1, source_target_pairs={{252,0},{0,4},{4,8},{8,12},{12,16},{16,20},{20,24},{24,28},{28,32}... | collective-permute-start | bytes 786440 | tf_op jit(solution)/shard_map/ppermute | solution.py:28
  367.6 21.5 %collective-permute-start.33 = (bf16[256,4,128]{0,2,1:T(8,128)(2,1)S(1)}, bf16[256,4,128]{0,2,1:T(8,128)(2,1)S(1)}, u32[]{:S(2)}, u32[]{:S(2)}) collective-permute-start(bf16[256,4,128]{0,2,1:T(8,128)(2,1)S(1)} %fusion.48), channel_id=1, source_target_pairs={{252,0},{0,4},{4,8},{8,12},{12,16},{16,20},{20,24},{24,28},{28,32}... | collective-permute-start | bytes 786440 | tf_op jit(solution)/shard_map/ppermute | solution.py:28
  382.1 16.0 %collective-permute-start.25 = (bf16[256,4,128]{0,2,1:T(8,128)(2,1)S(1)}, bf16[256,4,128]{0,2,1:T(8,128)(2,1)S(1)}, u32[]{:S(2)}, u32[]{:S(2)}) collective-permute-start(bf16[256,4,128]{0,2,1:T(8,128)(2,1)S(1)} %add_convert_fusion.8), channel_id=1, source_target_pairs={{252,0},{0,4},{4,8},{8,12},{12,16},{16,20},{20,24},{24,28},{28,32}... | collective-permute-start | bytes 786440 | tf_op jit(solution)/shard_map/ppermute | solution.py:28
  389.5 16.9 %collective-permute-start.34 = (bf16[256,4,128]{0,2,1:T(8,128)(2,1)S(1)}, bf16[256,4,128]{0,2,1:T(8,128)(2,1)S(1)}, u32[]{:S(2)}, u32[]{:S(2)}) collective-permute-start(bf16[256,4,128]{0,2,1:T(8,128)(2,1)S(1)} %add_convert_fusion), channel_id=1, source_target_pairs={{252,0},{0,4},{4,8},{8,12},{12,16},{16,20},{20,24},{24,28},{28,32}... | collective-permute-start | bytes 786440 | tf_op jit(solution)/shard_map/ppermute | solution.py:28
  398.2 15.7 %collective-permute-start.26 = (bf16[256,4,128]{0,2,1:T(8,128)(2,1)S(1)}, bf16[256,4,128]{0,2,1:T(8,128)(2,1)S(1)}, u32[]{:S(2)}, u32[]{:S(2)}) collective-permute-start(bf16[256,4,128]{0,2,1:T(8,128)(2,1)S(1)} %add_convert_fusion.7), channel_id=1, source_target_pairs={{252,0},{0,4},{4,8},{8,12},{12,16},{16,20},{20,24},{24,28},{28,32}... | collective-permute-start | bytes 786440 | tf_op jit(solution)/shard_map/ppermute | solution.py:28
  406.7 14.9 %collective-permute-start.35 = (bf16[256,4,128]{0,2,1:T(8,128)(2,1)S(1)}, bf16[256,4,128]{0,2,1:T(8,128)(2,1)S(1)}, u32[]{:S(2)}, u32[]{:S(2)}) collective-permute-start(bf16[256,4,128]{0,2,1:T(8,128)(2,1)S(1)} %fusion.132), channel_id=1, source_target_pairs={{252,0},{0,4},{4,8},{8,12},{12,16},{16,20},{20,24},{24,28},{28,32}... | collective-permute-start | bytes 786440 | tf_op jit(solution)/shard_map/ppermute | solution.py:28
  413.9 14.9 %collective-permute-start.27 = (bf16[256,4,128]{0,2,1:T(8,128)(2,1)S(1)}, bf16[256,4,128]{0,2,1:T(8,128)(2,1)S(1)}, u32[]{:S(2)}, u32[]{:S(2)}) collective-permute-start(bf16[256,4,128]{0,2,1:T(8,128)(2,1)S(1)} %add_convert_fusion.6), channel_id=1, source_target_pairs={{252,0},{0,4},{4,8},{8,12},{12,16},{16,20},{20,24},{24,28},{28,32}... | collective-permute-start | bytes 786440 | tf_op jit(solution)/shard_map/ppermute | solution.py:28
  (116 other events, 2469.2 us)
Sparse Core Ops, SparseCore 0:
  9.8 31.1 all-gather.2
  42.8 303.5 all-gather.4
  363.8 341.4 reduce-scatter.1
where the time goes:
time: 717 us; the launch traced here: 712 us
  waiting for transfers between devices  591 us (82%)
  starting transfers between devices  51.4 us (7%)
  matrix products  34.5 us (5%)
  between operations  15.8 us (2%)
  local copies, waits for them, and re-layouts  13 us (2%)
    reduce_scatter x1, waiting for transfers between devices, shards(): lax.psum_scatter(lax.dot_general(attention, grad_full, (((0,), (0,)), (()...  214 us
    all_gather x1, waiting for transfers between devices, shards(): lax.all_gather(out_weight, 'ctx', axis=0, tiled=True)  145 us
    ppermute x24, waiting for transfers between devices, shifted(): return lax.ppermute(array, axis, pairs)  128 us
    ppermute x18, waiting for transfers between devices, passed_along(): return lax.ppermute(block, axis, route)  102 us
    ppermute x24, starting transfers between devices, shifted(): return lax.ppermute(array, axis, pairs)  47.8 us
  transfers between devices with their start and end apart: 45, of which 41 were waited for; matrix products, arithmetic and copies ran while one was open for 6% of the time, Pallas kernels for 0%

commit v1 on v0

--- a/solution.py
+++ b/solution.py
@@ -86,7 +86,9 @@
     grad_full = lax.all_gather(grad_out, "fsdp", axis=1, tiled=True)
     grad_attn = lax.dot_general(
         grad_full,
-        lax.all_gather(out_weight, "ctx", axis=0, tiled=True),
+        jnp.concatenate(
+            lax.all_to_all(jnp.stack([out_weight] * lax.axis_size("ctx")), "ctx", 0, 0), axis=0
+        ),
         (((1,), (1,)), ((), ())),
         preferred_element_type=jnp.float32,
     ).astype(jnp.bfloat16)

time: 717 us -> 661 us (0.922)
  waiting for transfers between devices: 591 us -> 522 us
  starting transfers between devices: 51.4 us -> 63.1 us
    all_gather x1 -> x0, waiting for transfers between devices: 145 us -> none  [shards(): lax.all_gather(out_weight, 'ctx', axis=0, tiled=True)]
    ppermute x24, waiting for transfers between devices: 128 us -> 206 us  [shifted(): return lax.ppermute(array, axis, pairs)]
    all_to_all x0 -> x1, starting transfers between devices: none -> 13.4 us  [shards(): lax.all_to_all(jnp.stack([out_weight] * lax.axis_size('ctx')), 'ctx', 0, 0)]
    reduce_scatter x1, waiting for transfers between devices: 214 us -> 201 us  [shards(): lax.psum_scatter(lax.dot_general(attention, grad_full, (((0,), (0,)), (()...]
    ppermute x18, waiting for transfers between devices: 102 us -> 114 us  [passed_along(): return lax.ppermute(block, axis, route)]
  transfers between devices with their start and end apart: 45 -> 45, of which waited for: 41 -> 40; matrix products, arithmetic and copies ran while one was open for 6% -> 6% of each run, Pallas kernels for 0% -> 0%
where the time goes in v1:
time: 661 us; the launch traced here: 655 us
  waiting for transfers between devices  522 us (79%)
  starting transfers between devices  63.1 us (10%)
  matrix products  35.8 us (5%)
  between operations  16.4 us (2%)
  local copies, waits for them, and re-layouts  11.9 us (2%)
    ppermute x24, waiting for transfers between devices, shifted(): return lax.ppermute(array, axis, pairs)  206 us
    reduce_scatter x1, waiting for transfers between devices, shards(): lax.psum_scatter(lax.dot_general(attention, grad_full, (((0,), (0,)), (()...  201 us
    ppermute x18, waiting for transfers between devices, passed_along(): return lax.ppermute(block, axis, route)  114 us
    ppermute x24, starting transfers between devices, shifted(): return lax.ppermute(array, axis, pairs)  47.8 us
    all_to_all x1, starting transfers between devices, shards(): lax.all_to_all(jnp.stack([out_weight] * lax.axis_size('ctx')), 'ctx', 0, 0)  13.4 us
  transfers between devices with their start and end apart: 45, of which 40 were waited for; matrix products, arithmetic and copies ran while one was open for 6% of the time, Pallas kernels for 0%

profile of v1, /device:TPU:8, one launch (start us, length us, event | category | flops | bytes accessed | tf_op | source)
XLA Modules:
  0.0 654.8 jit_solution(9572235660674189667)
XLA Ops:
  10.6 13.4 %all-to-all-start = ((bf16[64,8,4096]{2,1,0:T(8,128)(2,1)}), bf16[64,8,4096]{2,1,0:T(8,128)(2,1)}, u32[]{:S(2)}, u32[]{:S(2)}) async-start(bf16[64,8,4096]{2,1,0:T(8,128)(2,1)} %stack.2), calls=%async_computation | async-start | bytes 8388608 | tf_op jit(solution)/shard_map/all_to_all | solution.py:90
  27.4 91.0 %collective-permute-done = s32[256]{0:T(256)S(1)} collective-permute-done((s32[256]{0:T(256)S(1)}, s32[256]{0:T(256)S(1)}, u32[]{:S(2)}, u32[]{:S(2)}) %collective-permute-start) | collective-permute-done | bytes 1056 | tf_op jit(solution)/shard_map/ppermute | solution.py:14
  120.3 7.8 %collective-permute-done.2 = s32[256]{0:T(256)S(1)} collective-permute-done((s32[256]{0:T(256)S(1)}, s32[256]{0:T(256)S(1)}, u32[]{:S(2)}, u32[]{:S(2)}) %collective-permute-start.2) | collective-permute-done | bytes 1056 | tf_op jit(solution)/shard_map/ppermute | solution.py:14
  139.7 7.7 %collective-permute-done.6 = s32[256]{0:T(256)S(1)} collective-permute-done((s32[256]{0:T(256)S(1)}, s32[256]{0:T(256)S(1)}, u32[]{:S(2)}, u32[]{:S(2)}) %collective-permute-start.6) | collective-permute-done | bytes 1056 | tf_op jit(solution)/shard_map/ppermute | solution.py:14
  149.4 7.7 %collective-permute-done.8 = s32[256]{0:T(256)S(1)} collective-permute-done((s32[256]{0:T(256)S(1)}, s32[256]{0:T(256)S(1)}, u32[]{:S(2)}, u32[]{:S(2)}) %collective-permute-start.8) | collective-permute-done | bytes 1056 | tf_op jit(solution)/shard_map/ppermute | solution.py:14
  159.1 7.7 %collective-permute-done.10 = s32[256]{0:T(256)S(1)} collective-permute-done((s32[256]{0:T(256)S(1)}, s32[256]{0:T(256)S(1)}, u32[]{:S(2)}, u32[]{:S(2)}) %collective-permute-start.10) | collective-permute-done | bytes 1056 | tf_op jit(solution)/shard_map/ppermute | solution.py:14
  168.7 7.7 %collective-permute-done.12 = s32[256]{0:T(256)S(1)} collective-permute-done((s32[256]{0:T(256)S(1)}, s32[256]{0:T(256)S(1)}, u32[]{:S(2)}, u32[]{:S(2)}) %collective-permute-start.12) | collective-permute-done | bytes 1056 | tf_op jit(solution)/shard_map/ppermute | solution.py:14
  178.4 7.8 %collective-permute-done.14 = s32[256]{0:T(256)S(1)} collective-permute-done((s32[256]{0:T(256)S(1)}, s32[256]{0:T(256)S(1)}, u32[]{:S(2)}, u32[]{:S(2)}) %collective-permute-start.14) | collective-permute-done | bytes 1056 | tf_op jit(solution)/shard_map/ppermute | solution.py:14
  191.7 11.0 %collective-permute-done.3 = bf16[256,4,128]{2,0,1:T(8,128)(2,1)S(1)} collective-permute-done((bf16[256,4,128]{2,0,1:T(8,128)(2,1)S(1)}, bf16[256,4,128]{2,0,1:T(8,128)(2,1)S(1)}, u32[]{:S(2)}, u32[]{:S(2)}) %collective-permute-start.3) | collective-permute-done | bytes 262176 | tf_op jit(solution)/shard_map/ppermute | solution.py:14
  210.6 6.8 %collective-permute-done.5 = bf16[256,4,128]{2,0,1:T(8,128)(2,1)S(1)} collective-permute-done((bf16[256,4,128]{2,0,1:T(8,128)(2,1)S(1)}, bf16[256,4,128]{2,0,1:T(8,128)(2,1)S(1)}, u32[]{:S(2)}, u32[]{:S(2)}) %collective-permute-start.5) | collective-permute-done | bytes 262176 | tf_op jit(solution)/shard_map/ppermute | solution.py:14
  322.1 5.9 collective-permute-done.24
  328.4 7.8 %collective-permute-done.33 = bf16[256,4,128]{0,2,1:T(8,128)(2,1)S(1)} collective-permute-done((bf16[256,4,128]{0,2,1:T(8,128)(2,1)S(1)}, bf16[256,4,128]{0,2,1:T(8,128)(2,1)S(1)}, u32[]{:S(2)}, u32[]{:S(2)}) %collective-permute-start.33) | collective-permute-done | bytes 262176 | tf_op jit(solution)/shard_map/ppermute | solution.py:28
  337.0 7.0 %collective-permute-done.25 = bf16[256,4,128]{0,2,1:T(8,128)(2,1)S(1)} collective-permute-done((bf16[256,4,128]{0,2,1:T(8,128)(2,1)S(1)}, bf16[256,4,128]{0,2,1:T(8,128)(2,1)S(1)}, u32[]{:S(2)}, u32[]{:S(2)}) %collective-permute-start.25) | collective-permute-done | bytes 262176 | tf_op jit(solution)/shard_map/ppermute | solution.py:28
  344.1 7.7 %collective-permute-done.34 = bf16[256,4,128]{0,2,1:T(8,128)(2,1)S(1)} collective-permute-done((bf16[256,4,128]{0,2,1:T(8,128)(2,1)S(1)}, bf16[256,4,128]{0,2,1:T(8,128)(2,1)S(1)}, u32[]{:S(2)}, u32[]{:S(2)}) %collective-permute-start.34) | collective-permute-done | bytes 262176 | tf_op jit(solution)/shard_map/ppermute | solution.py:28
  352.6 7.7 %collective-permute-done.26 = bf16[256,4,128]{0,2,1:T(8,128)(2,1)S(1)} collective-permute-done((bf16[256,4,128]{0,2,1:T(8,128)(2,1)S(1)}, bf16[256,4,128]{0,2,1:T(8,128)(2,1)S(1)}, u32[]{:S(2)}, u32[]{:S(2)}) %collective-permute-start.26) | collective-permute-done | bytes 262176 | tf_op jit(solution)/shard_map/ppermute | solution.py:28
  360.4 8.1 %collective-permute-done.35 = bf16[256,4,128]{0,2,1:T(8,128)(2,1)S(1)} collective-permute-done((bf16[256,4,128]{0,2,1:T(8,128)(2,1)S(1)}, bf16[256,4,128]{0,2,1:T(8,128)(2,1)S(1)}, u32[]{:S(2)}, u32[]{:S(2)}) %collective-permute-start.35) | collective-permute-done | bytes 262176 | tf_op jit(solution)/shard_map/ppermute | solution.py:28
  369.2 6.4 collective-permute-done.27
  376.0 7.5 %collective-permute-done.36 = bf16[256,4,128]{0,2,1:T(8,128)(2,1)S(1)} collective-permute-done((bf16[256,4,128]{0,2,1:T(8,128)(2,1)S(1)}, bf16[256,4,128]{0,2,1:T(8,128)(2,1)S(1)}, u32[]{:S(2)}, u32[]{:S(2)}) %collective-permute-start.36) | collective-permute-done | bytes 262176 | tf_op jit(solution)/shard_map/ppermute | solution.py:28
  384.2 7.9 %collective-permute-done.28 = bf16[256,4,128]{0,2,1:T(8,128)(2,1)S(1)} collective-permute-done((bf16[256,4,128]{0,2,1:T(8,128)(2,1)S(1)}, bf16[256,4,128]{0,2,1:T(8,128)(2,1)S(1)}, u32[]{:S(2)}, u32[]{:S(2)}) %collective-permute-start.28) | collective-permute-done | bytes 262176 | tf_op jit(solution)/shard_map/ppermute | solution.py:28
  392.2 8.2 %collective-permute-done.37 = bf16[256,4,128]{0,2,1:T(8,128)(2,1)S(1)} collective-permute-done((bf16[256,4,128]{0,2,1:T(8,128)(2,1)S(1)}, bf16[256,4,128]{0,2,1:T(8,128)(2,1)S(1)}, u32[]{:S(2)}, u32[]{:S(2)}) %collective-permute-start.37) | collective-permute-done | bytes 262176 | tf_op jit(solution)/shard_map/ppermute | solution.py:28
  401.2 7.1 %collective-permute-done.29 = bf16[256,4,128]{0,2,1:T(8,128)(2,1)S(1)} collective-permute-done((bf16[256,4,128]{0,2,1:T(8,128)(2,1)S(1)}, bf16[256,4,128]{0,2,1:T(8,128)(2,1)S(1)}, u32[]{:S(2)}, u32[]{:S(2)}) %collective-permute-start.29) | collective-permute-done | bytes 262176 | tf_op jit(solution)/shard_map/ppermute | solution.py:28
  408.4 6.4 collective-permute-done.38
  426.6 7.1 %collective-permute-done.31 = bf16[256,4,128]{0,2,1:T(8,128)(2,1)S(1)} collective-permute-done((bf16[256,4,128]{0,2,1:T(8,128)(2,1)S(1)}, bf16[256,4,128]{0,2,1:T(8,128)(2,1)S(1)}, u32[]{:S(2)}, u32[]{:S(2)}) %collective-permute-start.31) | collective-permute-done | bytes 262176 | tf_op jit(solution)/shard_map/ppermute | solution.py:28
  446.5 201.2 %reduce-scatter.2.cloned.1.call-done = f32[8,4096]{1,0:T(8,128)} async-done(((f32[512,4096]{1,0:T(8,128)}), f32[8,4096]{1,0:T(8,128)}) %reduce-scatter.2.cloned.1.call-update) | async-done | bytes 131088 | tf_op jit(solution)/shard_map/reduce_scatter | solution.py:95
  (354 shorter events, 173.9 us)
Async XLA Ops:
  10.6 281.0 %all-to-all-start = ((bf16[64,8,4096]{2,1,0:T(8,128)(2,1)}), bf16[64,8,4096]{2,1,0:T(8,128)(2,1)}, u32[]{:S(2)}, u32[]{:S(2)}) async-start(bf16[64,8,4096]{2,1,0:T(8,128)(2,1)} %stack.2), calls=%async_computation | async-start | bytes 8388608 | tf_op jit(solution)/shard_map/all_to_all | solution.py:90
  24.0 267.7 %all-gather.2.cloned.1.call-start = ((), (), s32[]{:S(2)}) async-start(), calls=%async_computation.2 | async-start | bytes 2621440 | tf_op jit(solution)/shard_map/all_gather | solution.py:86
  24.0 94.4 %collective-permute-start = (s32[256]{0:T(256)S(1)}, s32[256]{0:T(256)S(1)}, u32[]{:S(2)}, u32[]{:S(2)}) collective-permute-start(s32[256]{0:T(256)S(1)} %broadcast_add_fusion), channel_id=1, source_target_pairs={{0,4},{4,8},{8,12},{12,16},{16,20},{20,24},{24,28},{28,32},{32,36}... | collective-permute-start | bytes 3080 | tf_op jit(solution)/shard_map/ppermute | solution.py:14
  130.0 517.7 %reduce-scatter.2.cloned.1.call-start = ((), (), s32[]{:S(2)}) async-start(), calls=%async_computation.3 | async-start | bytes 8519680 | tf_op jit(solution)/shard_map/reduce_scatter | solution.py:95
  130.4 57.0 %collective-permute-start.1 = (bf16[256,4,128]{2,0,1:T(8,128)(2,1)S(1)}, bf16[256,4,128]{2,0,1:T(8,128)(2,1)S(1)}, u32[]{:S(2)}, u32[]{:S(2)}) collective-permute-start(bf16[256,4,128]{2,0,1:T(8,128)(2,1)S(1)} %copy.116), channel_id=1, source_target_pairs={{0,4},{4,8},{8,12},{12,16},{16,20},{20,24},{24,28},{28,32},{32,36}... | collective-permute-start | bytes 786440 | tf_op jit(solution)/shard_map/ppermute | solution.py:14
  132.5 56.9 %collective-permute-start.16 = (bf16[256,4,128]{0,2,1:T(8,128)(2,1)S(1)}, bf16[256,4,128]{0,2,1:T(8,128)(2,1)S(1)}, u32[]{:S(2)}, u32[]{:S(2)}) collective-permute-start(bf16[256,4,128]{0,2,1:T(8,128)(2,1)S(1)} %bitcast.470), channel_id=1, source_target_pairs={{0,4},{4,8},{8,12},{12,16},{16,20},{20,24},{24,28},{28,32},{32,36}... | collective-permute-start | bytes 786440 | tf_op jit(solution)/shard_map/ppermute | solution.py:14
  187.4 15.2 %collective-permute-start.3 = (bf16[256,4,128]{2,0,1:T(8,128)(2,1)S(1)}, bf16[256,4,128]{2,0,1:T(8,128)(2,1)S(1)}, u32[]{:S(2)}, u32[]{:S(2)}) collective-permute-start(bf16[256,4,128]{2,0,1:T(8,128)(2,1)S(1)} %collective-permute-done.1), channel_id=1, source_target_pairs={{0,4},{4,8},{8,12},{12,16},{16,20},{20,24},{24,28},{28,32},{32,36}... | collective-permute-start | bytes 786440 | tf_op jit(solution)/shard_map/ppermute | solution.py:14
  189.4 18.9 %collective-permute-start.17 = (bf16[256,4,128]{0,2,1:T(8,128)(2,1)S(1)}, bf16[256,4,128]{0,2,1:T(8,128)(2,1)S(1)}, u32[]{:S(2)}, u32[]{:S(2)}) collective-permute-start(bf16[256,4,128]{0,2,1:T(8,128)(2,1)S(1)} %collective-permute-done.16), channel_id=1, source_target_pairs={{0,4},{4,8},{8,12},{12,16},{16,20},{20,24},{24,28},{28,32},{32,36}... | collective-permute-start | bytes 786440 | tf_op jit(solution)/shard_map/ppermute | solution.py:14
  202.7 14.6 %collective-permute-start.5 = (bf16[256,4,128]{2,0,1:T(8,128)(2,1)S(1)}, bf16[256,4,128]{2,0,1:T(8,128)(2,1)S(1)}, u32[]{:S(2)}, u32[]{:S(2)}) collective-permute-start(bf16[256,4,128]{2,0,1:T(8,128)(2,1)S(1)} %collective-permute-done.3), channel_id=1, source_target_pairs={{0,4},{4,8},{8,12},{12,16},{16,20},{20,24},{24,28},{28,32},{32,36}... | collective-permute-start | bytes 786440 | tf_op jit(solution)/shard_map/ppermute | solution.py:14
  208.3 14.5 %collective-permute-start.18 = (bf16[256,4,128]{0,2,1:T(8,128)(2,1)S(1)}, bf16[256,4,128]{0,2,1:T(8,128)(2,1)S(1)}, u32[]{:S(2)}, u32[]{:S(2)}) collective-permute-start(bf16[256,4,128]{0,2,1:T(8,128)(2,1)S(1)} %collective-permute-done.17), channel_id=1, source_target_pairs={{0,4},{4,8},{8,12},{12,16},{16,20},{20,24},{24,28},{28,32},{32,36}... | collective-permute-start | bytes 786440 | tf_op jit(solution)/shard_map/ppermute | solution.py:14
  256.5 13.7 %collective-permute-start.13 = (bf16[256,4,128]{2,0,1:T(8,128)(2,1)S(1)}, bf16[256,4,128]{2,0,1:T(8,128)(2,1)S(1)}, u32[]{:S(2)}, u32[]{:S(2)}) collective-permute-start(bf16[256,4,128]{2,0,1:T(8,128)(2,1)S(1)} %collective-permute-done.11), channel_id=1, source_target_pairs={{0,4},{4,8},{8,12},{12,16},{16,20},{20,24},{24,28},{28,32},{32,36}... | collective-permute-start | bytes 786440 | tf_op jit(solution)/shard_map/ppermute | solution.py:14
  275.0 27.0 %collective-permute-start.23 = (bf16[256,4,128]{0,2,1:T(8,128)(2,1)}, bf16[256,4,128]{0,2,1:T(8,128)(2,1)}, u32[]{:S(2)}, u32[]{:S(2)}) collective-permute-start(bf16[256,4,128]{0,2,1:T(8,128)(2,1)} %collective-permute-done.22), channel_id=1, source_target_pairs={{0,4},{4,8},{8,12},{12,16},{16,20},{20,24},{24,28},{28,32},{32,36}... | collective-permute-start | bytes 786440 | tf_op jit(solution)/shard_map/ppermute | solution.py:14
  312.1 15.9 %collective-permute-start.24 = (bf16[256,4,128]{0,2,1:T(8,128)(2,1)S(1)}, bf16[256,4,128]{0,2,1:T(8,128)(2,1)S(1)}, u32[]{:S(2)}, u32[]{:S(2)}) collective-permute-start(bf16[256,4,128]{0,2,1:T(8,128)(2,1)S(1)} %fusion.54), channel_id=1, source_target_pairs={{252,0},{0,4},{4,8},{8,12},{12,16},{16,20},{20,24},{24,28},{28,32}... | collective-permute-start | bytes 786440 | tf_op jit(solution)/shard_map/ppermute | solution.py:28
  313.8 22.4 %collective-permute-start.33 = (bf16[256,4,128]{0,2,1:T(8,128)(2,1)S(1)}, bf16[256,4,128]{0,2,1:T(8,128)(2,1)S(1)}, u32[]{:S(2)}, u32[]{:S(2)}) collective-permute-start(bf16[256,4,128]{0,2,1:T(8,128)(2,1)S(1)} %fusion.53), channel_id=1, source_target_pairs={{252,0},{0,4},{4,8},{8,12},{12,16},{16,20},{20,24},{24,28},{28,32}... | collective-permute-start | bytes 786440 | tf_op jit(solution)/shard_map/ppermute | solution.py:28
  328.3 15.7 %collective-permute-start.25 = (bf16[256,4,128]{0,2,1:T(8,128)(2,1)S(1)}, bf16[256,4,128]{0,2,1:T(8,128)(2,1)S(1)}, u32[]{:S(2)}, u32[]{:S(2)}) collective-permute-start(bf16[256,4,128]{0,2,1:T(8,128)(2,1)S(1)} %add_convert_fusion.8), channel_id=1, source_target_pairs={{252,0},{0,4},{4,8},{8,12},{12,16},{16,20},{20,24},{24,28},{28,32}... | collective-permute-start | bytes 786440 | tf_op jit(solution)/shard_map/ppermute | solution.py:28
  336.6 15.2 %collective-permute-start.34 = (bf16[256,4,128]{0,2,1:T(8,128)(2,1)S(1)}, bf16[256,4,128]{0,2,1:T(8,128)(2,1)S(1)}, u32[]{:S(2)}, u32[]{:S(2)}) collective-permute-start(bf16[256,4,128]{0,2,1:T(8,128)(2,1)S(1)} %add_convert_fusion), channel_id=1, source_target_pairs={{252,0},{0,4},{4,8},{8,12},{12,16},{16,20},{20,24},{24,28},{28,32}... | collective-permute-start | bytes 786440 | tf_op jit(solution)/shard_map/ppermute | solution.py:28
  344.1 16.2 %collective-permute-start.26 = (bf16[256,4,128]{0,2,1:T(8,128)(2,1)S(1)}, bf16[256,4,128]{0,2,1:T(8,128)(2,1)S(1)}, u32[]{:S(2)}, u32[]{:S(2)}) collective-permute-start(bf16[256,4,128]{0,2,1:T(8,128)(2,1)S(1)} %add_convert_fusion.7), channel_id=1, source_target_pairs={{252,0},{0,4},{4,8},{8,12},{12,16},{16,20},{20,24},{24,28},{28,32}... | collective-permute-start | bytes 786440 | tf_op jit(solution)/shard_map/ppermute | solution.py:28
  352.1 16.3 %collective-permute-start.35 = (bf16[256,4,128]{0,2,1:T(8,128)(2,1)S(1)}, bf16[256,4,128]{0,2,1:T(8,128)(2,1)S(1)}, u32[]{:S(2)}, u32[]{:S(2)}) collective-permute-start(bf16[256,4,128]{0,2,1:T(8,128)(2,1)S(1)} %fusion.137), channel_id=1, source_target_pairs={{252,0},{0,4},{4,8},{8,12},{12,16},{16,20},{20,24},{24,28},{28,32}... | collective-permute-start | bytes 786440 | tf_op jit(solution)/shard_map/ppermute | solution.py:28
  360.3 15.4 %collective-permute-start.27 = (bf16[256,4,128]{0,2,1:T(8,128)(2,1)S(1)}, bf16[256,4,128]{0,2,1:T(8,128)(2,1)S(1)}, u32[]{:S(2)}, u32[]{:S(2)}) collective-permute-start(bf16[256,4,128]{0,2,1:T(8,128)(2,1)S(1)} %add_convert_fusion.6), channel_id=1, source_target_pairs={{252,0},{0,4},{4,8},{8,12},{12,16},{16,20},{20,24},{24,28},{28,32}... | collective-permute-start | bytes 786440 | tf_op jit(solution)/shard_map/ppermute | solution.py:28
  368.8 14.7 %collective-permute-start.36 = (bf16[256,4,128]{0,2,1:T(8,128)(2,1)S(1)}, bf16[256,4,128]{0,2,1:T(8,128)(2,1)S(1)}, u32[]{:S(2)}, u32[]{:S(2)}) collective-permute-start(bf16[256,4,128]{0,2,1:T(8,128)(2,1)S(1)} %fusion.130), channel_id=1, source_target_pairs={{252,0},{0,4},{4,8},{8,12},{12,16},{16,20},{20,24},{24,28},{28,32}... | collective-permute-start | bytes 786440 | tf_op jit(solution)/shard_map/ppermute | solution.py:28
  375.7 16.4 %collective-permute-start.28 = (bf16[256,4,128]{0,2,1:T(8,128)(2,1)S(1)}, bf16[256,4,128]{0,2,1:T(8,128)(2,1)S(1)}, u32[]{:S(2)}, u32[]{:S(2)}) collective-permute-start(bf16[256,4,128]{0,2,1:T(8,128)(2,1)S(1)} %add_convert_fusion.5), channel_id=1, source_target_pairs={{252,0},{0,4},{4,8},{8,12},{12,16},{16,20},{20,24},{24,28},{28,32}... | collective-permute-start | bytes 786440 | tf_op jit(solution)/shard_map/ppermute | solution.py:28
  383.8 16.6 %collective-permute-start.37 = (bf16[256,4,128]{0,2,1:T(8,128)(2,1)S(1)}, bf16[256,4,128]{0,2,1:T(8,128)(2,1)S(1)}, u32[]{:S(2)}, u32[]{:S(2)}) collective-permute-start(bf16[256,4,128]{0,2,1:T(8,128)(2,1)S(1)} %fusion.123), channel_id=1, source_target_pairs={{252,0},{0,4},{4,8},{8,12},{12,16},{16,20},{20,24},{24,28},{28,32}... | collective-permute-start | bytes 786440 | tf_op jit(solution)/shard_map/ppermute | solution.py:28
  392.2 16.1 %collective-permute-start.29 = (bf16[256,4,128]{0,2,1:T(8,128)(2,1)S(1)}, bf16[256,4,128]{0,2,1:T(8,128)(2,1)S(1)}, u32[]{:S(2)}, u32[]{:S(2)}) collective-permute-start(bf16[256,4,128]{0,2,1:T(8,128)(2,1)S(1)} %add_convert_fusion.4), channel_id=1, source_target_pairs={{252,0},{0,4},{4,8},{8,12},{12,16},{16,20},{20,24},{24,28},{28,32}... | collective-permute-start | bytes 786440 | tf_op jit(solution)/shard_map/ppermute | solution.py:28
  400.8 14.1 %collective-permute-start.38 = (bf16[256,4,128]{0,2,1:T(8,128)(2,1)S(1)}, bf16[256,4,128]{0,2,1:T(8,128)(2,1)S(1)}, u32[]{:S(2)}, u32[]{:S(2)}) collective-permute-start(bf16[256,4,128]{0,2,1:T(8,128)(2,1)S(1)} %fusion.116), channel_id=1, source_target_pairs={{252,0},{0,4},{4,8},{8,12},{12,16},{16,20},{20,24},{24,28},{28,32}... | collective-permute-start | bytes 786440 | tf_op jit(solution)/shard_map/ppermute | solution.py:28
  (117 other events, 2822.4 us)
Sparse Core Ops, SparseCore 0:
  130.1 27.5 all-gather.1
  308.9 338.7 reduce-scatter.1
